TPU v7x, 512 devices: a whole 4x8x8 slice. The times are simulated.
512 devices in a mesh: grp: 8 (over y_lo, core), own: 64 (over x, y_hi, z).
Axes of the slice: x: 4, y: 8 (y_hi: 2, y_lo: 4; y = y_hi * 4 + y_lo), z: 8, core: 2. Of those that a mesh axis runs over, the one named last changes fastest.
Arguments:
- activations: bfloat16 [65536, 1024], P(('grp', 'own'))
- out_grads: bfloat16 [65536, 1024], P(('grp', 'own')), may hold values from -0.01953125 to 0.01953125
- master: float32 [1024, 1024], P('own'), may hold values from -6 to 6
- moment: float32 [1024, 1024], P('own'), may hold values from 0.05 to 5
- left_root: bfloat16 [1024, 1024], P('own'), may hold values from -0.25 to 2.25, as said below
- right_root: bfloat16 [1024, 1024], P('own'), may hold values from -0.25 to 2.25, as said below
- stats_in: float32 [256, 16, 1024], P('own'), may hold values from -6 to 6
- tile_slot: int32 [128], replicated, may hold values from 0 to 255, as said below
Outputs:
- master_out: float32 [1024, 1024], P('own')
- moment_out: float32 [1024, 1024], P('own')
- stats_out: float32 [256, 16, 1024], P('own')
- weights: bfloat16 [1024, 1024], replicated
Inputs may be any that keep to these rules, and one draw needn't show every extreme that they name: `tile_slot`: distinct slot numbers; slot s belongs to owner s // 4; some owner holds 4 tiles. `left_root`: symmetric. `right_root`: symmetric.
All inputs are finite; a program needn't handle non-finite values.
Results may differ from a plain program's by a relative error of at most 0.005.
Values may be sent and summed in bfloat16 or wider, within the bound.
No kernel may reach another device: no remote copies, remote signals or barrier semaphores. Data moves between devices by JAX's collectives and lax.ppermute only.
A program may use at most 64 MiB of HBM per device.

v0:
```python
import jax
import jax.numpy as jnp
from jax import lax
from jax.sharding import PartitionSpec as P

stat_decay = 0.9
moment_decay = 0.95
learn_rate = 0.3
adam_eps = 1e-08
norm_eps = 1e-06


def local(activations, out_grads, master, moment, left_root, right_root, stats_in, tile_slot):
    owner_rows = master.shape[0]
    block_size = master.shape[1]
    capacity = stats_in.shape[0]
    tile_rows = stats_in.shape[1]
    tile_count = tile_slot.shape[0]
    owner_index = lax.axis_index("own")
    gradient = lax.psum(
        lax.dot_general(
            activations, out_grads, (((0,), (0,)), ((), ())), preferred_element_type=jnp.float32
        ),
        ("grp", "own"),
    )
    grad_rows = lax.dynamic_slice_in_dim(gradient, owner_index * owner_rows, owner_rows, 0)
    moment_out = moment_decay * moment + (1.0 - moment_decay) * grad_rows * grad_rows
    adam_dir = grad_rows / (jnp.sqrt(moment_out) + adam_eps)
    my_slots = owner_index * capacity + jnp.arange(capacity, dtype=jnp.int32)
    matches = (tile_slot[:, None] == my_slots[None, :]).astype(jnp.int32)
    tile_ids = jnp.sum(matches * jnp.arange(tile_count, dtype=jnp.int32)[:, None], axis=0)
    filled = jnp.sum(matches, axis=0)
    per_half = block_size // tile_rows

    def slot_update(packed):
        tile_id, slot_filled, old_tile = packed
        which_half = tile_id // per_half
        offset = (tile_id - which_half * per_half) * tile_rows

        def left_product():
            row_block = lax.dynamic_slice_in_dim(gradient, offset, tile_rows, 0)
            return lax.dot_general(
                row_block,
                gradient,
                (((1,), (1,)), ((), ())),
                precision=lax.Precision.HIGHEST,
                preferred_element_type=jnp.float32,
            )

        def right_product():
            column_block = lax.dynamic_slice_in_dim(gradient, offset, tile_rows, 1)
            return lax.dot_general(
                column_block,
                gradient,
                (((0,), (0,)), ((), ())),
                precision=lax.Precision.HIGHEST,
                preferred_element_type=jnp.float32,
            )

        product = lax.cond(which_half == 0, left_product, right_product)
        return jnp.where(
            slot_filled > 0, stat_decay * old_tile + (1.0 - stat_decay) / block_size * product, 0.0
        )

    stats_out = lax.map(slot_update, (tile_ids, filled, stats_in))
    grad_low = gradient.astype(jnp.bfloat16)
    left_mid = jnp.dot(left_root, grad_low, preferred_element_type=jnp.float32).astype(jnp.bfloat16)
    precond = jnp.dot(
        left_mid,
        lax.all_gather(right_root, "own", axis=0, tiled=True),
        preferred_element_type=jnp.float32,
    )
    adam_sum, precond_sum = lax.psum(
        (jnp.sum(adam_dir * adam_dir), jnp.sum(precond * precond)), "own"
    )
    graft_scale = jnp.sqrt(adam_sum) / (jnp.sqrt(precond_sum) + norm_eps)
    master_out = master - learn_rate * graft_scale * precond
    weights = lax.all_gather(master_out.astype(jnp.bfloat16), "own", axis=0, tiled=True)
    return (master_out, moment_out, stats_out, weights)


def solution(mesh):
    in_specs = (
        P(("grp", "own"), None),
        P(("grp", "own"), None),
        P("own", None),
        P("own", None),
        P("own", None),
        P("own", None),
        P("own", None, None),
        P(),
    )
    out_specs = (P("own", None), P("own", None), P("own", None, None), P())
    return jax.shard_map(local, mesh=mesh, in_specs=in_specs, out_specs=out_specs, check_vma=False)
```

profile of v0, /device:TPU:8, one launch (start us, length us, event | category | flops | bytes accessed | tf_op | source)
XLA Modules:
  0.0 686.9 jit_solution(6704430149430638157)
XLA Ops:
  8.1 0.9 copy-done
  9.0 3.6 fusion.22
  12.7 0.5 all-gather.3.cloned.1.call-update
  13.3 305.9 %all-reduce.3.cloned.1.call-done = f32[1024,1024]{1,0:T(8,128)} async-done(((f32[1024,1024]{1,0:T(8,128)}), f32[1024,1024]{1,0:T(8,128)}) %all-reduce.3.cloned.1.call-update) | async-done | bytes 4194320 | tf_op jit(solution)/shard_map/psum | solution.py:20
  319.2 2.1 multiply_reduce_fusion.1
  321.3 4.9 multiply_reduce_fusion
  326.2 221.8 %all-reduce = (f32[]{:T(128)}, f32[]{:T(128)}) all-reduce(f32[]{:T(128)} %get-tuple-element.119, f32[]{:T(128)} %get-tuple-element.121), channel_id=1, replica_groups=mesh['grp'=8,'own'=64] {'own'}, use_global_device_ids=true, to_apply=%region_2.0 | all-reduce | flops 2 | bytes 16 | tf_op jit(solution)/shard_map/psum | solution.py:73
  549.5 0.6 fusion.18
  550.2 0.2 fusion.17
  550.3 50.1 %while.12 = (s32[]{:T(128)}, f32[4,16,1024]{2,1,0:T(8,128)}, s32[4]{0:T(128)S(1)}, f32[4,16,1024]{2,1,0:T(8,128)}, s32[4]{0:T(128)S(1)}, /*index=5*/f32[1024,102...) while((s32[]{:T(128)}, f32[4,16,1024]{2,1,0:T(8,128)}, ...), condition=%wide.region_10.11_spmd, body=%wide.region_7.10_spmd.sunk | while | flops 201392144 | bytes 4982188 | solution.py:65
  550.4 0.7 dynamic_slice.42
  554.5 4.8 conditional.2
  554.5 4.8 fusion
  559.3 0.7 dynamic_slice.43
  560.6 1.5 bitcast_dynamic-update-slice_fusion.2
  562.1 0.7 dynamic_slice.42
  566.3 5.8 conditional.2
  566.3 5.8 fusion.3
  572.1 0.7 dynamic_slice.43
  573.4 1.5 bitcast_dynamic-update-slice_fusion.2
  574.9 0.7 dynamic_slice.42
  579.1 5.8 conditional.2
  579.1 5.8 fusion.3
  584.8 0.7 dynamic_slice.43
  586.2 1.5 bitcast_dynamic-update-slice_fusion.2
  587.7 0.7 dynamic_slice.42
  591.8 5.8 conditional.2
  591.9 5.8 fusion.3
  597.6 0.7 dynamic_slice.43
  599.0 1.5 bitcast_dynamic-update-slice_fusion.2
  600.5 75.9 %all-gather.5.cloned.1.call-done = bf16[1024,1024]{1,0:T(8,128)(2,1)} async-done(((bf16[16,1024]{1,0:T(8,128)(2,1)}), bf16[1024,1024]{1,0:T(8,128)(2,1)}) %all-gather.5.cloned.1.call-update) | async-done | bytes 2097168 | tf_op jit(solution)/shard_map/all_gather | solution.py:78
  676.4 3.1 copy.23
  (17 shorter events, 0.2 us)
Async XLA Ops:
  8.0 1.0 copy-start
  8.0 311.2 %copy-start.1 = (f32[16,1024]{1,0:T(8,128)S(1)}, f32[16,1024]{1,0:T(8,128)}, u32[]{:S(2)}) copy-start(f32[16,1024]{1,0:T(8,128)} %param.15) | copy-start | bytes 196612
  8.0 313.3 %copy-start.3 = (bf16[16,1024]{1,0:T(8,128)(2,1)S(1)}, bf16[16,1024]{1,0:T(8,128)(2,1)}, u32[]{:S(2)}) copy-start(bf16[16,1024]{1,0:T(8,128)(2,1)} %param.16) | copy-start | bytes 98308
  8.0 311.2 %all-reduce.3.cloned.1.call-start = ((), (), s32[]{:S(2)}) async-start(), calls=%async_computation | async-start | bytes 8388608 | tf_op jit(solution)/shard_map/psum | solution.py:20
  12.6 536.8 %copy-start.2 = (f32[16,1024]{1,0:T(8,128)S(1)}, f32[16,1024]{1,0:T(8,128)}, u32[]{:S(2)}) copy-start(f32[16,1024]{1,0:T(8,128)} %param.14) | copy-start | bytes 196612
  12.6 537.5 %copy-start.4 = (s32[128]{0:T(128)S(1)}, s32[128]{0:T(128)}, u32[]{:S(2)}) copy-start(s32[128]{0:T(128)} %param.19) | copy-start | bytes 1540
  12.6 308.7 %all-gather.3.cloned.1.call-start = ((), (), s32[]{:S(2)}) async-start(), calls=%async_computation.1 | async-start | bytes 2129920 | tf_op jit(solution)/shard_map/all_gather | solution.py:70
  13.2 663.2 %all-gather.5.cloned.1.call-start = ((), (), s32[]{:S(2)}) async-start(), calls=%async_computation.2 | async-start | bytes 2129920 | tf_op jit(solution)/shard_map/all_gather | solution.py:78
Sparse Core Ops, SparseCore 0:
  13.8 305.3 all-reduce.2
Sparse Core Ops, SparseCore 1:
  17.7 140.6 all-gather.2
  550.2 126.2 all-gather.4
where the time goes:
time: 688 us; the launch traced here: 687 us
  waiting for transfers between devices  382 us (56%)
  blocking collectives  222 us (32%)
  matrix products  30.6 us (4%)
  between operations  17 us (2%)
  loops' own time  16.8 us (2%)
  local copies, waits for them, and re-layouts  9.33 us (1%)
  other arithmetic  8.89 us (1%)
    psum x1, waiting for transfers between devices, local(): lax.psum(lax.dot_general(activations, out_grads, (((0,), (0,)), ((), ()))...  306 us
    psum x1, blocking collectives, local(): lax.psum((jnp.sum(adam_dir * adam_dir), jnp.sum(precond * precond)), 'own')  222 us
    all_gather x1, waiting for transfers between devices, local(): lax.all_gather(master_out.astype(jnp.bfloat16), 'own', axis=0, tiled=True)  75.9 us
    dot_general x3, matrix products, left_product(): lax.dot_general(row_block, gradient, (((1,), (1,)), ((), ())), precision=...  17.3 us
    another operation x1, loops' own time, local(): stats_out = lax.map(slot_update, (tile_ids, filled, stats_in))  16.7 us
  transfers between devices with their start and end apart: 3, of which 2 were waited for; matrix products, arithmetic and copies ran while one was open for 5% of the time, Pallas kernels for 0%

commit v1 on v0

--- a/solution.py
+++ b/solution.py
@@ -1,3 +1,4 @@
+import functools
 import jax
 import jax.numpy as jnp
 from jax import lax
@@ -8,6 +9,15 @@
 learn_rate = 0.3
 adam_eps = 1e-08
 norm_eps = 1e-06
+
+
+def _save_vector(base_x, mesh_dim, at_axis):
+    fresh = jnp.stack([base_x for _ in range(lax.axis_size(mesh_dim))], 0)
+    part_next = lax.all_to_all(fresh, mesh_dim, 0, 0)
+    return jnp.concatenate(part_next, at_axis)
+
+
+manage_set_in = functools.partial(_save_vector, mesh_dim="own", at_axis=0)
 
 
 def local(activations, out_grads, master, moment, left_root, right_root, stats_in, tile_slot):
@@ -75,7 +85,7 @@
     )
     graft_scale = jnp.sqrt(adam_sum) / (jnp.sqrt(precond_sum) + norm_eps)
     master_out = master - learn_rate * graft_scale * precond
-    weights = lax.all_gather(master_out.astype(jnp.bfloat16), "own", axis=0, tiled=True)
+    weights = manage_set_in(master_out.astype(jnp.bfloat16))
     return (master_out, moment_out, stats_out, weights)
 
 

time: 688 us -> 622 us (0.904)
  the two profiles are of different devices: /device:TPU:8 before, /device:TPU:60 now
where the time goes in v1:
time: 622 us; the launch traced here: 621 us
  waiting for transfers between devices  307 us (49%)
  blocking collectives  185 us (30%)
  starting transfers between devices  49.4 us (8%)
  matrix products  31.6 us (5%)
  between operations  17 us (3%)
  loops' own time  13.6 us (2%)
  other arithmetic  8.88 us (1%)
  local copies, waits for them, and re-layouts  8.46 us (1%)
    psum x1, waiting for transfers between devices, local(): lax.psum(lax.dot_general(activations, out_grads, (((0,), (0,)), ((), ()))...  307 us
    psum x1, blocking collectives, local(): lax.psum((jnp.sum(adam_dir * adam_dir), jnp.sum(precond * precond)), 'own')  185 us
    all_to_all x1, starting transfers between devices, _save_vector(): part_next = lax.all_to_all(fresh, mesh_dim, 0, 0)  49.3 us
    dot_general x4, matrix products, left_product(): lax.dot_general(row_block, gradient, (((1,), (1,)), ((), ())), precision=...  23 us
    another operation x1, loops' own time, local(): stats_out = lax.map(slot_update, (tile_ids, filled, stats_in))  13.5 us
  transfers between devices with their start and end apart: 3, of which 1 were waited for; matrix products, arithmetic and copies ran while one was open for 6% of the time, Pallas kernels for 0%

profile of v1, /device:TPU:60, one launch (start us, length us, event | category | flops | bytes accessed | tf_op | source)
XLA Modules:
  0.0 621.0 jit_solution(14956953409244939951)
XLA Ops:
  8.1 0.9 copy-done
  9.0 3.7 fusion.22
  12.7 0.5 all-gather.2.cloned.1.call-update
  13.2 306.7 %all-reduce.3.cloned.1.call-done = f32[1024,1024]{1,0:T(8,128)} async-done(((f32[1024,1024]{1,0:T(8,128)}), f32[1024,1024]{1,0:T(8,128)}) %all-reduce.3.cloned.1.call-update) | async-done | bytes 4194320 | tf_op jit(solution)/shard_map/psum | solution.py:30
  320.0 2.1 multiply_reduce_fusion.1
  322.1 4.9 multiply_reduce_fusion
  327.0 184.7 %all-reduce = (f32[]{:T(128)}, f32[]{:T(128)}) all-reduce(f32[]{:T(128)} %get-tuple-element.119, f32[]{:T(128)} %get-tuple-element.121), channel_id=1, replica_groups=mesh['grp'=8,'own'=64] {'own'}, use_global_device_ids=true, to_apply=%region_2.0 | all-reduce | flops 2 | bytes 16 | tf_op jit(solution)/shard_map/psum | solution.py:83
  513.2 0.6 fusion.18
  513.8 1.6 stack.2
  515.4 49.3 %all-to-all-start = ((bf16[64,16,1024]{2,1,0:T(8,128)(2,1)}), bf16[64,16,1024]{2,1,0:T(8,128)(2,1)S(1)}, u32[]{:S(2)}, u32[]{:S(2)}) async-start(bf16[64,16,1024]{2,1,0:T(8,128)(2,1)} %stack.2), calls=%async_computation | async-start | bytes 4194304 | tf_op jit(solution)/shard_map/all_to_all | solution.py:16
  564.9 47.3 %while.12 = (s32[]{:T(128)}, f32[4,16,1024]{2,1,0:T(8,128)}, s32[4]{0:T(128)S(1)}, f32[4,16,1024]{2,1,0:T(8,128)}, s32[4]{0:T(128)S(1)}, /*index=5*/f32[1024,102...) while((s32[]{:T(128)}, f32[4,16,1024]{2,1,0:T(8,128)}, ...), condition=%wide.region_10.11_spmd, body=%wide.region_7.10_spmd.sunk | while | flops 201392144 | bytes 4982188 | solution.py:75
  564.9 0.6 dynamic_slice.42
  568.3 5.8 conditional.2
  568.4 5.8 fusion.3
  574.1 0.6 dynamic_slice.43
  575.3 1.5 bitcast_dynamic-update-slice_fusion.2
  576.8 0.6 dynamic_slice.42
  580.1 5.8 conditional.2
  580.2 5.8 fusion.3
  585.9 0.6 dynamic_slice.43
  587.1 1.5 bitcast_dynamic-update-slice_fusion.2
  588.6 0.6 dynamic_slice.42
  592.0 5.8 conditional.2
  592.0 5.8 fusion.3
  597.7 0.6 dynamic_slice.43
  598.9 1.5 bitcast_dynamic-update-slice_fusion.2
  600.4 0.6 dynamic_slice.42
  603.8 5.8 conditional.2
  603.8 5.8 fusion.3
  609.6 0.6 dynamic_slice.43
  610.7 1.5 bitcast_dynamic-update-slice_fusion.2
  612.2 1.3 copy.23
  (17 shorter events, 0.3 us)
Async XLA Ops:
  8.0 1.0 copy-start
  8.0 311.9 %copy-start.1 = (f32[16,1024]{1,0:T(8,128)S(1)}, f32[16,1024]{1,0:T(8,128)}, u32[]{:S(2)}) copy-start(f32[16,1024]{1,0:T(8,128)} %param.15) | copy-start | bytes 196612
  8.0 314.0 %copy-start.3 = (bf16[16,1024]{1,0:T(8,128)(2,1)S(1)}, bf16[16,1024]{1,0:T(8,128)(2,1)}, u32[]{:S(2)}) copy-start(bf16[16,1024]{1,0:T(8,128)(2,1)} %param.16) | copy-start | bytes 98308
  8.0 311.9 %all-reduce.3.cloned.1.call-start = ((), (), s32[]{:S(2)}) async-start(), calls=%async_computation.1 | async-start | bytes 8388608 | tf_op jit(solution)/shard_map/psum | solution.py:30
  12.6 500.5 %copy-start.2 = (f32[16,1024]{1,0:T(8,128)S(1)}, f32[16,1024]{1,0:T(8,128)}, u32[]{:S(2)}) copy-start(f32[16,1024]{1,0:T(8,128)} %param.14) | copy-start | bytes 196612
  12.6 309.4 %all-gather.2.cloned.1.call-start = ((), (), s32[]{:S(2)}) async-start(), calls=%async_computation.2 | async-start | bytes 2129920 | tf_op jit(solution)/shard_map/all_gather | solution.py:80
  327.0 237.8 %copy-start.4 = (s32[128]{0:T(128)S(1)}, s32[128]{0:T(128)}, u32[]{:S(2)}) copy-start(s32[128]{0:T(128)} %param.19) | copy-start | bytes 1540
  515.4 96.8 %all-to-all-start = ((bf16[64,16,1024]{2,1,0:T(8,128)(2,1)}), bf16[64,16,1024]{2,1,0:T(8,128)(2,1)S(1)}, u32[]{:S(2)}, u32[]{:S(2)}) async-start(bf16[64,16,1024]{2,1,0:T(8,128)(2,1)} %stack.2), calls=%async_computation | async-start | bytes 4194304 | tf_op jit(solution)/shard_map/all_to_all | solution.py:16
Sparse Core Ops, SparseCore 0:
  13.8 306.0 all-reduce.2
Sparse Core Ops, SparseCore 1:
  17.7 136.0 all-gather.1
